TPU v7x, 512 devices: a whole 4x4x16 slice. The times are simulated.
512 devices in a mesh: row: 64 (over z, x), rep: 8 (over y, core).
Axes of the slice: x: 4, y: 4, z: 16, core: 2. Of those that a mesh axis runs over, the one named last changes fastest.
Arguments:
- features: bfloat16 [16384, 128], P('row', 'rep'), may hold values from -6 to 6
- owner_index: int32 [16384], P('row'), may hold values from 0 to 16383, as said below
- block_cols: int32 [128, 64], P('row', 'rep'), may hold values from 0 to 127, as said below
- block_count: int32 [128], P('row'), may hold values from 1 to 64, as said below
- tiles: bfloat16 [128, 64, 128, 128], P('row', 'rep'), may hold values from -0.109375 to 0.109375
- weight: bfloat16 [128, 256], P(None, 'rep'), may hold values from -0.75 to 0.75
- bias: float32 [256], P('rep'), may hold values from -4 to 4
- grad_out: bfloat16 [16384, 256], P('row', 'rep'), may hold values from -6 to 6
Outputs:
- hidden: bfloat16 [16384, 256], P('row', 'rep')
- weight_grad: float32 [128, 256], P(None, 'rep')
- bias_grad: float32 [256], P('rep')
Inputs may be any that keep to these rules, and one draw needn't show every extreme that they name: `owner_index`: A permutation; the 256 rows of each loader shard hold exactly 4 positions of every partition's 2*128 rows. `block_cols`: the block columns of one block row are distinct. Block column c belongs to partition c // 2. Over all slots of one partition's 2 block rows, exactly 1 distinct block columns of each partition are named. `block_count`: some block row has all 64 slots live.
All inputs are finite; a program needn't handle non-finite values.
Results may differ from a plain program's by a relative error of at most 0.017.
Values may be sent and summed in bfloat16 or wider, within the bound.
No kernel may reach another device: no remote copies, remote signals or barrier semaphores. Data moves between devices by JAX's collectives and lax.ppermute only.
A program may use at most 64 MiB of HBM per device.

v0:
```python
import jax
import jax.numpy as jnp
from jax import lax
from jax.sharding import PartitionSpec as P


def sum_over(x, axis_name, count):
    rows = x.shape[0]
    pieces = x.reshape((count, rows // count) + x.shape[1:])
    got = lax.all_to_all(pieces, axis_name, 0, 0, tiled=True)
    reduced = jnp.sum(got.astype(jnp.float32), axis=0)
    return reduced


def spread(x, axis_name, count):
    wide = jnp.broadcast_to(x[None], (count,) + x.shape)
    return lax.all_to_all(wide, axis_name, 0, 0, tiled=True)


def on_device(features, owner_index, block_cols, block_count, tiles, weight, bias, grad_out):
    rows_part, cols_dev = features.shape
    parts = lax.axis_size("row")
    reps = lax.axis_size("rep")
    per_pair = rows_part // parts
    rb, slots_dev, size_blk = (tiles.shape[0], tiles.shape[1], tiles.shape[2])
    destination = owner_index // rows_part
    same = destination[:, None] == destination[None, :]
    before = jnp.arange(rows_part)[:, None] > jnp.arange(rows_part)[None, :]
    rank = jnp.sum(same & before, axis=1)
    slot = rank * parts + destination
    place = (slot[:, None] == jnp.arange(rows_part)[None, :]).astype(jnp.bfloat16)
    pos_row = (owner_index % rows_part).astype(jnp.bfloat16)
    loader = jnp.concatenate([features.T, pos_row[None, :]], axis=0)
    packet = jnp.dot(loader, place, preferred_element_type=jnp.float32).astype(jnp.bfloat16)
    width = cols_dev + 1
    packet = packet.reshape(width, per_pair, parts)
    wide = jnp.broadcast_to(packet[None], (parts,) + packet.shape)
    grouped = lax.all_to_all(wide, "row", 0, 2, tiled=True)[0]
    pos = grouped[cols_dev].T.astype(jnp.int32)
    values = grouped[:cols_dev]
    cols_all = lax.all_gather(block_cols, "rep", axis=1, tiled=True)
    part_of = cols_all // rb
    half_of = cols_all % rb
    part_ids = jnp.arange(parts, dtype=jnp.int32)
    hit = part_of[None, :, :] == part_ids[:, None, None]
    half = jnp.max(jnp.where(hit, half_of[None, :, :], 0), axis=(1, 2))
    node_ids = jnp.arange(size_blk, dtype=jnp.int32)
    target = half[:, None, None] * size_blk + node_ids[None, None, :]
    pick = (pos[:, :, None] == target).astype(jnp.bfloat16)
    needed = jnp.einsum("fgq,qgn->qfn", grouped, pick, preferred_element_type=jnp.float32).astype(
        jnp.bfloat16
    )
    needed = needed[:, :cols_dev, :]
    peer_parts = part_of.reshape(rb, reps, slots_dev).transpose(1, 0, 2).reshape(-1)
    choose = (peer_parts[:, None] == part_ids[None, :]).astype(jnp.bfloat16)
    outgoing = jnp.dot(choose, needed.reshape(parts, -1), preferred_element_type=jnp.float32)
    outgoing = outgoing.astype(jnp.bfloat16).reshape(reps, rb, slots_dev, cols_dev, size_blk)
    incoming = lax.all_to_all(outgoing, "rep", 0, 0, tiled=True)
    slot_ids = lax.axis_index("rep") * slots_dev + jnp.arange(slots_dev, dtype=jnp.int32)
    live = slot_ids[None, :] < block_count[:, None]
    tiles_live = jnp.where(live[:, :, None, None], tiles, jnp.zeros_like(tiles))
    partial = jnp.einsum(
        "rsin,jrsfn->rijf", tiles_live, incoming, preferred_element_type=jnp.float32
    )
    partial = partial.reshape(rows_part, reps * cols_dev)
    shares = spread(partial.astype(jnp.bfloat16), "rep", reps)
    agg = jnp.sum(shares.astype(jnp.float32), axis=0).astype(jnp.bfloat16)
    pre = jnp.dot(agg, weight, preferred_element_type=jnp.float32) + bias
    hidden = jax.nn.silu(pre).astype(jnp.bfloat16)
    sig = jax.nn.sigmoid(pre)
    dpre = (grad_out.astype(jnp.float32) * sig * (1.0 + pre * (1.0 - sig))).astype(jnp.bfloat16)
    weight_term = jnp.dot(agg.T, dpre, preferred_element_type=jnp.float32)
    bias_term = jnp.sum(dpre.astype(jnp.float32), axis=0)
    n_in, n_out = weight_term.shape
    bias_row = jnp.pad(bias_term, (0, n_in - n_out))[None, :]
    stacked = jnp.concatenate([weight_term.T, bias_row], axis=0)
    per = -(-stacked.shape[0] // parts)
    stacked = jnp.pad(stacked, ((0, parts * per - stacked.shape[0]), (0, 0)))
    total = spread(sum_over(stacked, "row", parts), "row", parts).reshape(parts * per, n_in)
    weight_grad = total[:n_out].T
    bias_grad = total[n_out, :n_out]
    return (hidden, weight_grad, bias_grad)


def solution(mesh):
    placed = (
        P("row", "rep"),
        P("row"),
        P("row", "rep"),
        P("row"),
        P("row", "rep", None, None),
        P(None, "rep"),
        P("rep"),
        P("row", "rep"),
    )
    return jax.shard_map(
        on_device,
        mesh=mesh,
        in_specs=placed,
        out_specs=(P("row", "rep"), P(None, "rep"), P("rep")),
        check_vma=False,
    )
```

profile of v0, /device:TPU:8, one launch (start us, length us, event | category | flops | bytes accessed | tf_op | source)
XLA Modules:
  0.0 133.0 jit_solution(4461811390317609364)
XLA Ops:
  0.6 0.7 fusion.18
  1.3 0.2 convert_reduce_fusion
  1.5 0.9 convolution_convert_fusion.1
  2.6 0.3 broadcast_in_dim.38
  2.9 1.6 %reshape.116 = bf16[64,2,2176]{2,1,0:T(2,128)(2,1)} reshape(bf16[64,17,4,64]{3,2,1,0:T(4,128)(2,1)S(1)} %broadcast_in_dim.38) | data formatting | bytes 1114112
  4.5 18.6 %all-to-all-start = ((bf16[64,2,2176]{2,1,0:T(2,128)(2,1)}), bf16[64,2,2176]{2,1,0:T(2,128)(2,1)S(1)}, u32[]{:S(2)}, u32[]{:S(2)}) async-start(bf16[64,2,2176]{2,1,0:T(2,128)(2,1)} %reshape.116), calls=%async_computation | async-start | bytes 1114112 | tf_op jit(solution)/shard_map/all_to_all | solution.py:38
  23.0 8.8 %all-gather = s32[8,8,2]{1,2,0:T(2,128)S(1)} all-gather(s32[1,8,2]{1,2,0:T(2,128)S(1)} %bitcast.85), channel_id=1, replica_groups=mesh['row'=64,'rep'=8] {'rep'}, dimensions={0}, use_global_device_ids=true | all-gather | bytes 576 | tf_op jit(solution)/shard_map/all_gather | solution.py:41
  32.3 25.0 %all-to-all-done = bf16[64,2,2176]{2,1,0:T(2,128)(2,1)S(1)} async-done(((bf16[64,2,2176]{2,1,0:T(2,128)(2,1)}), bf16[64,2,2176]{2,1,0:T(2,128)(2,1)S(1)}, u32[]{:S(2)}, u32[]{:S(2)}) %all-to-all-start) | async-done | bytes 557088 | tf_op jit(solution)/shard_map/all_to_all | solution.py:38
  57.3 0.7 reshape.117
  58.0 0.5 copy.34
  58.5 0.8 copy.36
  59.5 3.7 %fusion = bf16[64,17,128]{2,1,0:T(8,128)(2,1)S(1)} fusion(bf16[17,256,64]{1,0,2:T(8,128)(2,1)S(1)} %copy.36, s32[64,128]{1,0:T(8,128)S(1)} %iota_add_fusion, s32[64,256]{1,0:T(8,128)S(1)} %copy.35), kind=kOutput, calls=%fused_computation | convolution fusion | flops 73400320 | bytes 933888 | tf_op jit(solution)/shard_map/fgq,qgn->qfn/dot_general | solution.py:50
  63.3 0.3 convolution_convert_fusion
  63.6 0.9 copy.37
  64.5 4.9 %all-to-all-start.1 = ((bf16[8,2,8,16,128]{4,3,2,1,0:T(8,128)(2,1)}), bf16[8,2,8,16,128]{4,3,2,1,0:T(8,128)(2,1)S(1)}, u32[]{:S(2)}, u32[]{:S(2)}) async-start(bf16[8,2,8,16,128]{4,3,2,1,0:T(8,128)(2,1)} %copy.37), calls=%async_computation.1 | async-start | bytes 1048576 | tf_op jit(solution)/shard_map/all_to_all | solution.py:58
  69.5 8.8 %all-to-all-done.1 = bf16[8,2,8,16,128]{4,3,2,1,0:T(8,128)(2,1)S(1)} async-done(((bf16[8,2,8,16,128]{4,3,2,1,0:T(8,128)(2,1)}), bf16[8,2,8,16,128]{4,3,2,1,0:T(8,128)(2,1)S(1)}, u32[]{:S(2)}, u32[]{:S(2)}) %all-to-all-start.1) | async-done | bytes 524320 | tf_op jit(solution)/shard_map/all_to_all | solution.py:58
  78.3 0.4 fusion.4
  79.0 12.8 %all_to_all.35 = bf16[8,256,128]{2,1,0:T(8,128)(2,1)S(1)} all-to-all(bf16[8,256,128]{2,1,0:T(8,128)(2,1)S(1)} %broadcast_in_dim.41), channel_id=1, replica_groups=mesh['row'=64,'rep'=8] {'rep'}, dimensions={0} | all-to-all | bytes 1048576 | tf_op jit(solution)/shard_map/all_to_all | solution.py:17
  92.0 0.9 convert_reduce_fusion.1
  92.8 0.1 fusion.21
  93.0 20.2 %all_to_all.36 = f32[64,1,128]{2,1,0:T(1,128)S(1)} all-to-all(f32[64,1,128]{2,1,0:T(1,128)S(1)} %bitcast.81), channel_id=1, replica_groups=mesh['row'=64,'rep'=8] {'row'}, dimensions={0} | all-to-all | bytes 65536 | tf_op jit(solution)/shard_map/all_to_all | solution.py:10
  113.3 18.5 %all_to_all.37 = f32[64,1,128]{2,1,0:T(1,128)S(1)} all-to-all(f32[64,1,128]{2,1,0:T(1,128)S(1)} %broadcast_in_dim.43), channel_id=1, replica_groups=mesh['row'=64,'rep'=8] {'row'}, dimensions={0} | all-to-all | bytes 65536 | tf_op jit(solution)/shard_map/all_to_all | solution.py:17
  131.8 0.5 slice_bitcast_fusion
  132.4 0.6 slice.23
  (39 shorter events, 1.3 us)
Async XLA Ops:
  0.6 91.3 %copy-start = (bf16[128,32]{0,1:T(8,128)(2,1)S(1)}, bf16[128,32]{0,1:T(8,128)(2,1)}, u32[]{:S(2)}) copy-start(bf16[128,32]{0,1:T(8,128)(2,1)} %param.13) | copy-start | bytes 24580
  2.9 20.2 %copy-start.1 = (s32[2,8]{1,0:T(2,128)S(1)}, s32[2,8]{1,0:T(2,128)}, u32[]{:S(2)}) copy-start(s32[2,8]{1,0:T(2,128)} %param.10) | copy-start | bytes 196
  4.5 52.8 %all-to-all-start = ((bf16[64,2,2176]{2,1,0:T(2,128)(2,1)}), bf16[64,2,2176]{2,1,0:T(2,128)(2,1)S(1)}, u32[]{:S(2)}, u32[]{:S(2)}) async-start(bf16[64,2,2176]{2,1,0:T(2,128)(2,1)} %reshape.116), calls=%async_computation | async-start | bytes 1114112 | tf_op jit(solution)/shard_map/all_to_all | solution.py:38
  63.6 5.8 %copy-start.4 = (s32[2]{0:T(128)S(1)}, s32[2]{0:T(128)}, u32[]{:S(2)}) copy-start(s32[2]{0:T(128)} %param.11) | copy-start | bytes 28
  63.6 14.7 %copy-start.2 = (bf16[2,8,128,128]{3,2,1,0:T(8,128)(2,1)S(1)}, bf16[2,8,128,128]{3,2,1,0:T(8,128)(2,1)}, u32[]{:S(2)}) copy-start(bf16[2,8,128,128]{3,2,1,0:T(8,128)(2,1)} %param.12) | copy-start | bytes 1572868
  64.5 13.8 %all-to-all-start.1 = ((bf16[8,2,8,16,128]{4,3,2,1,0:T(8,128)(2,1)}), bf16[8,2,8,16,128]{4,3,2,1,0:T(8,128)(2,1)S(1)}, u32[]{:S(2)}, u32[]{:S(2)}) async-start(bf16[8,2,8,16,128]{4,3,2,1,0:T(8,128)(2,1)} %copy.37), calls=%async_computation.1 | async-start | bytes 1048576 | tf_op jit(solution)/shard_map/all_to_all | solution.py:58
  78.9 13.0 %copy-start.3 = (bf16[256,32]{0,1:T(8,128)(2,1)S(1)}, bf16[256,32]{0,1:T(8,128)(2,1)}, u32[]{:S(2)}) copy-start(bf16[256,32]{0,1:T(8,128)(2,1)} %param.15) | copy-start | bytes 49156
  78.9 13.0 %copy-start.5 = (f32[32]{0:T(128)S(1)}, f32[32]{0:T(128)}, u32[]{:S(2)}) copy-start(f32[32]{0:T(128)} %param.14) | copy-start | bytes 388
where the time goes:
time: 133 us
  blocking collectives  60.3 us (45%)
  waiting for transfers between devices  33.8 us (25%)
  starting transfers between devices  23.5 us (18%)
  local copies, waits for them, and re-layouts  6.78 us (5%)
  matrix products  6.39 us (5%)
  other arithmetic  1.35 us (1%)
    all_to_all x2, blocking collectives, spread(): return lax.all_to_all(wide, axis_name, 0, 0, tiled=True)  31.3 us
    all_to_all x1, waiting for transfers between devices, on_device(): grouped = lax.all_to_all(wide, 'row', 0, 2, tiled=True)[0]  25 us
    all_to_all x1, blocking collectives, sum_over(): got = lax.all_to_all(pieces, axis_name, 0, 0, tiled=True)  20.2 us
    all_to_all x1, starting transfers between devices, on_device(): grouped = lax.all_to_all(wide, 'row', 0, 2, tiled=True)[0]  18.6 us
    all_to_all x1, waiting for transfers between devices, on_device(): incoming = lax.all_to_all(outgoing, 'rep', 0, 0, tiled=True)  8.81 us
    all_gather x1, blocking collectives, on_device(): cols_all = lax.all_gather(block_cols, 'rep', axis=1, tiled=True)  8.77 us
    all_to_all x1, starting transfers between devices, on_device(): incoming = lax.all_to_all(outgoing, 'rep', 0, 0, tiled=True)  4.92 us
    dot_general x1, matrix products, on_device(): jnp.einsum('fgq,qgn->qfn', grouped, pick, preferred_element_type=jnp.floa...  3.74 us
  transfers between devices with their start and end apart: 2, of which 2 were waited for; matrix products, arithmetic and copies ran while one was open for 0% of the time, Pallas kernels for 0%

commit v1 on v0

--- a/solution.py
+++ b/solution.py
@@ -38,7 +38,9 @@
     grouped = lax.all_to_all(wide, "row", 0, 2, tiled=True)[0]
     pos = grouped[cols_dev].T.astype(jnp.int32)
     values = grouped[:cols_dev]
-    cols_all = lax.all_gather(block_cols, "rep", axis=1, tiled=True)
+    cols_all = jnp.concatenate(
+        lax.all_to_all(jnp.stack([block_cols] * lax.axis_size("rep")), "rep", 0, 0), axis=1
+    )
     part_of = cols_all // rb
     half_of = cols_all % rb
     part_ids = jnp.arange(parts, dtype=jnp.int32)

time: 133 us -> 140 us (1.053)
  waiting for transfers between devices: 33.8 us -> 42.9 us
  blocking collectives: 60.3 us -> 51.6 us
  starting transfers between devices: 23.5 us -> 28.3 us
    all_to_all x1, waiting for transfers between devices: 25 us -> 34.1 us  [on_device(): grouped = lax.all_to_all(wide, 'row', 0, 2, tiled=True)[0]]
    all_to_all x0 -> x1, starting transfers between devices: none -> 9.07 us  [on_device(): lax.all_to_all(jnp.stack([block_cols] * lax.axis_size('rep')), 'rep', 0, 0)]
    all_gather x1 -> x0, blocking collectives: 8.77 us -> none  [on_device(): cols_all = lax.all_gather(block_cols, 'rep', axis=1, tiled=True)]
    all_to_all x1, starting transfers between devices: 18.6 us -> 14.4 us  [on_device(): grouped = lax.all_to_all(wide, 'row', 0, 2, tiled=True)[0]]
  transfers between devices with their start and end apart: 2 -> 3, of which waited for: 2 -> 3; matrix products, arithmetic and copies ran while one was open for 0% -> 3% of each run, Pallas kernels for 0% -> 0%
where the time goes in v1:
time: 140 us; the launch traced here: 139 us
  blocking collectives  51.6 us (37%)
  waiting for transfers between devices  42.9 us (31%)
  starting transfers between devices  28.3 us (20%)
  local copies, waits for them, and re-layouts  7.96 us (6%)
  matrix products  6.39 us (5%)
    all_to_all x1, waiting for transfers between devices, on_device(): grouped = lax.all_to_all(wide, 'row', 0, 2, tiled=True)[0]  34.1 us
    all_to_all x2, blocking collectives, spread(): return lax.all_to_all(wide, axis_name, 0, 0, tiled=True)  31.3 us
    all_to_all x1, blocking collectives, sum_over(): got = lax.all_to_all(pieces, axis_name, 0, 0, tiled=True)  20.2 us
    all_to_all x1, starting transfers between devices, on_device(): grouped = lax.all_to_all(wide, 'row', 0, 2, tiled=True)[0]  14.4 us
    all_to_all x1, starting transfers between devices, on_device(): lax.all_to_all(jnp.stack([block_cols] * lax.axis_size('rep')), 'rep', 0, 0)  9.07 us
    all_to_all x1, waiting for transfers between devices, on_device(): incoming = lax.all_to_all(outgoing, 'rep', 0, 0, tiled=True)  8.81 us
    all_to_all x1, starting transfers between devices, on_device(): incoming = lax.all_to_all(outgoing, 'rep', 0, 0, tiled=True)  4.8 us
    dot_general x1, matrix products, on_device(): jnp.einsum('fgq,qgn->qfn', grouped, pick, preferred_element_type=jnp.floa...  3.74 us
  transfers between devices with their start and end apart: 3, of which 3 were waited for; matrix products, arithmetic and copies ran while one was open for 3% of the time, Pallas kernels for 0%

profile of v1, /device:TPU:8, one launch (start us, length us, event | category | flops | bytes accessed | tf_op | source)
XLA Modules:
  0.0 139.4 jit_solution(7016408110530962927)
XLA Ops:
  0.6 1.3 stack.2
  1.9 9.1 %all-to-all-start = ((s32[8,2,8]{2,1,0:T(2,128)}), s32[8,2,8]{2,1,0:T(2,128)S(1)}, u32[]{:S(2)}, u32[]{:S(2)}) async-start(s32[8,2,8]{2,1,0:T(2,128)} %stack.2), calls=%async_computation | async-start | bytes 16384 | tf_op jit(solution)/shard_map/all_to_all | solution.py:42
  11.0 0.7 fusion.18
  11.7 0.2 convert_reduce_fusion
  11.9 0.9 convolution_convert_fusion.1
  12.9 0.3 broadcast_in_dim.38
  13.2 1.6 %reshape.168 = bf16[64,2,2176]{2,1,0:T(2,128)(2,1)} reshape(bf16[64,17,4,64]{3,2,1,0:T(4,128)(2,1)S(1)} %broadcast_in_dim.38) | data formatting | bytes 1114112
  14.9 14.4 %all-to-all-start.1 = ((bf16[64,2,2176]{2,1,0:T(2,128)(2,1)}), bf16[64,2,2176]{2,1,0:T(2,128)(2,1)S(1)}, u32[]{:S(2)}, u32[]{:S(2)}) async-start(bf16[64,2,2176]{2,1,0:T(2,128)(2,1)} %reshape.168), calls=%async_computation.1 | async-start | bytes 1114112 | tf_op jit(solution)/shard_map/all_to_all | solution.py:38
  29.7 34.1 %all-to-all-done.1 = bf16[64,2,2176]{2,1,0:T(2,128)(2,1)S(1)} async-done(((bf16[64,2,2176]{2,1,0:T(2,128)(2,1)}), bf16[64,2,2176]{2,1,0:T(2,128)(2,1)S(1)}, u32[]{:S(2)}, u32[]{:S(2)}) %all-to-all-start.1) | async-done | bytes 557088 | tf_op jit(solution)/shard_map/all_to_all | solution.py:38
  63.8 0.7 reshape.169
  64.5 0.5 copy.29
  65.0 0.8 copy.32
  66.0 3.7 %fusion = bf16[64,17,128]{2,1,0:T(8,128)(2,1)S(1)} fusion(bf16[17,256,64]{1,0,2:T(8,128)(2,1)S(1)} %copy.32, s32[64,128]{1,0:T(8,128)S(1)} %iota_add_fusion, s32[64,256]{1,0:T(8,128)S(1)} %copy.30), kind=kOutput, calls=%fused_computation | convolution fusion | flops 73400320 | bytes 933888 | tf_op jit(solution)/shard_map/fgq,qgn->qfn/dot_general | solution.py:52
  69.8 0.3 convolution_convert_fusion
  70.1 0.9 copy.33
  71.0 4.8 %all-to-all-start.2 = ((bf16[8,2,8,16,128]{4,3,2,1,0:T(8,128)(2,1)}), bf16[8,2,8,16,128]{4,3,2,1,0:T(8,128)(2,1)S(1)}, u32[]{:S(2)}, u32[]{:S(2)}) async-start(bf16[8,2,8,16,128]{4,3,2,1,0:T(8,128)(2,1)} %copy.33), calls=%async_computation.2 | async-start | bytes 1048576 | tf_op jit(solution)/shard_map/all_to_all | solution.py:60
  75.9 8.8 %all-to-all-done.2 = bf16[8,2,8,16,128]{4,3,2,1,0:T(8,128)(2,1)S(1)} async-done(((bf16[8,2,8,16,128]{4,3,2,1,0:T(8,128)(2,1)}), bf16[8,2,8,16,128]{4,3,2,1,0:T(8,128)(2,1)S(1)}, u32[]{:S(2)}, u32[]{:S(2)}) %all-to-all-start.2) | async-done | bytes 524320 | tf_op jit(solution)/shard_map/all_to_all | solution.py:60
  84.7 0.4 fusion.4
  85.4 12.8 %all_to_all.40 = bf16[8,256,128]{2,1,0:T(8,128)(2,1)S(1)} all-to-all(bf16[8,256,128]{2,1,0:T(8,128)(2,1)S(1)} %broadcast_in_dim.41), channel_id=1, replica_groups=mesh['row'=64,'rep'=8] {'rep'}, dimensions={0} | all-to-all | bytes 1048576 | tf_op jit(solution)/shard_map/all_to_all | solution.py:17
  98.3 0.9 convert_reduce_fusion.1
  99.4 20.2 %all_to_all.41 = f32[64,1,128]{2,1,0:T(1,128)S(1)} all-to-all(f32[64,1,128]{2,1,0:T(1,128)S(1)} %bitcast.56), channel_id=1, replica_groups=mesh['row'=64,'rep'=8] {'row'}, dimensions={0} | all-to-all | bytes 65536 | tf_op jit(solution)/shard_map/all_to_all | solution.py:10
  119.7 18.5 %all_to_all.42 = f32[64,1,128]{2,1,0:T(1,128)S(1)} all-to-all(f32[64,1,128]{2,1,0:T(1,128)S(1)} %broadcast_in_dim.43), channel_id=1, replica_groups=mesh['row'=64,'rep'=8] {'row'}, dimensions={0} | all-to-all | bytes 65536 | tf_op jit(solution)/shard_map/all_to_all | solution.py:17
  138.2 0.5 slice_bitcast_fusion
  138.7 0.6 slice.23
  (38 shorter events, 1.4 us)
Async XLA Ops:
  0.6 97.7 %copy-start = (bf16[128,32]{0,1:T(8,128)(2,1)S(1)}, bf16[128,32]{0,1:T(8,128)(2,1)}, u32[]{:S(2)}) copy-start(bf16[128,32]{0,1:T(8,128)(2,1)} %param.13) | copy-start | bytes 24580
  1.9 12.9 %all-to-all-start = ((s32[8,2,8]{2,1,0:T(2,128)}), s32[8,2,8]{2,1,0:T(2,128)S(1)}, u32[]{:S(2)}, u32[]{:S(2)}) async-start(s32[8,2,8]{2,1,0:T(2,128)} %stack.2), calls=%async_computation | async-start | bytes 16384 | tf_op jit(solution)/shard_map/all_to_all | solution.py:42
  14.9 48.9 %all-to-all-start.1 = ((bf16[64,2,2176]{2,1,0:T(2,128)(2,1)}), bf16[64,2,2176]{2,1,0:T(2,128)(2,1)S(1)}, u32[]{:S(2)}, u32[]{:S(2)}) async-start(bf16[64,2,2176]{2,1,0:T(2,128)(2,1)} %reshape.168), calls=%async_computation.1 | async-start | bytes 1114112 | tf_op jit(solution)/shard_map/all_to_all | solution.py:38
  70.1 5.7 %copy-start.3 = (s32[2]{0:T(128)S(1)}, s32[2]{0:T(128)}, u32[]{:S(2)}) copy-start(s32[2]{0:T(128)} %param.11) | copy-start | bytes 28
  70.1 14.6 %copy-start.1 = (bf16[2,8,128,128]{3,2,1,0:T(8,128)(2,1)S(1)}, bf16[2,8,128,128]{3,2,1,0:T(8,128)(2,1)}, u32[]{:S(2)}) copy-start(bf16[2,8,128,128]{3,2,1,0:T(8,128)(2,1)} %param.12) | copy-start | bytes 1572868
  71.0 13.7 %all-to-all-start.2 = ((bf16[8,2,8,16,128]{4,3,2,1,0:T(8,128)(2,1)}), bf16[8,2,8,16,128]{4,3,2,1,0:T(8,128)(2,1)S(1)}, u32[]{:S(2)}, u32[]{:S(2)}) async-start(bf16[8,2,8,16,128]{4,3,2,1,0:T(8,128)(2,1)} %copy.33), calls=%async_computation.2 | async-start | bytes 1048576 | tf_op jit(solution)/shard_map/all_to_all | solution.py:60
  85.3 13.0 %copy-start.2 = (bf16[256,32]{0,1:T(8,128)(2,1)S(1)}, bf16[256,32]{0,1:T(8,128)(2,1)}, u32[]{:S(2)}) copy-start(bf16[256,32]{0,1:T(8,128)(2,1)} %param.15) | copy-start | bytes 49156
  85.3 13.0 %copy-start.4 = (f32[32]{0:T(128)S(1)}, f32[32]{0:T(128)}, u32[]{:S(2)}) copy-start(f32[32]{0:T(128)} %param.14) | copy-start | bytes 388
